TPU v7x, 256 devices: a whole 4x4x8 slice. The times are simulated.
256 devices in a mesh: section: 16 (over y, x), dp: 16 (over z, core).
Axes of the slice: x: 4, y: 4, z: 8, core: 2. Of those that a mesh axis runs over, the one named last changes fastest.
Arguments:
- hidden: bfloat16 [16, 256, 8192], P('dp', 'section'), may hold values from -1500 to 1500
- head: bfloat16 [65536, 8192], P('section', 'dp'), may hold values from -0.0625 to 0.0625
- block_id: int32 [16, 16], P(None, 'section'), may hold values from 0 to 7
- block_live: int32 [16, 16], P(None, 'section'), may hold values from 0 to 1, as said below
- teacher: bfloat16 [16, 256, 8192], P('dp', None, 'section'), may hold values from -400 to 400
Outputs:
- grad_hidden: bfloat16 [16, 256, 8192], P('dp', 'section')
- grad_head: bfloat16 [65536, 8192], P('section', 'dp')
Inputs may be any that keep to these rules, and one draw needn't show every extreme that they name: `block_live`: every micro-batch has at least one live section.
All inputs are finite; a program needn't handle non-finite values.
Results may differ from a plain program's by a relative error of at most 0.0056.
Values may be sent and summed in bfloat16 or wider, within the bound.
No kernel may reach another device: no remote copies, remote signals or barrier semaphores. Data moves between devices by JAX's collectives and lax.ppermute only.
A program may use at most 128 MiB of HBM per device.

v0:
```python
import jax
import jax.numpy as jnp
from jax import lax
from jax.sharding import PartitionSpec as P

neg_fill = -1e30


def local(hidden, head, block_id, block_live, teacher):
    my_replica = lax.axis_index("dp")
    n_dp = lax.axis_size("dp")
    tok_local = hidden.shape[1]
    model_width = hidden.shape[2]
    block_rows = teacher.shape[2]
    col_width = head.shape[1]
    blocks = head.shape[0] // block_rows
    table = head.reshape(blocks, block_rows, col_width)
    block_ids = block_id[:, 0]
    live_flags = block_live[:, 0]
    n_mb = block_ids.shape[0]
    pieces = hidden.reshape(1, tok_local, n_dp, col_width)
    pieces = lax.all_to_all(pieces, "dp", split_axis=2, concat_axis=0, tiled=True)
    hid_w = lax.all_gather(pieces, "section", axis=1, tiled=True).reshape(n_mb, -1, col_width)
    picked = jnp.take(table, block_ids, axis=0)
    part = jnp.einsum("mtw,mrw->mtr", hid_w, picked, preferred_element_type=jnp.float32)
    logits = lax.psum_scatter(part, "dp", scatter_dimension=0, tiled=True)[0]
    own_live = lax.dynamic_index_in_dim(live_flags, my_replica, 0, keepdims=False) > 0
    teach = teacher[0].astype(jnp.float32)
    live_value = jnp.where(own_live, 1.0, 0.0).astype(jnp.float32)
    stud_local = jnp.where(own_live, jnp.max(logits, axis=1), neg_fill)
    teach_local = jnp.where(own_live, jnp.max(teach, axis=1), neg_fill)
    stud_top, teach_top = lax.pmax((stud_local, teach_local), "section")
    stud_part = jnp.where(own_live, jnp.sum(jnp.exp(logits - stud_top[:, None]), axis=1), 0.0)
    teach_part = jnp.where(own_live, jnp.sum(jnp.exp(teach - teach_top[:, None]), axis=1), 0.0)
    stud_total, teach_total, live_count = lax.psum((stud_part, teach_part, live_value), "section")
    student = jnp.where(own_live, jnp.exp(logits - stud_top[:, None]) / stud_total[:, None], 0.0)
    teach_prob = jnp.where(
        own_live, jnp.exp(teach - teach_top[:, None]) / teach_total[:, None], 0.0
    )
    logit_grad = (block_rows * live_count * (student - teach_prob)).astype(jnp.bfloat16)
    grads = lax.all_gather(logit_grad[None], "dp", axis=0, tiled=True)
    contrib = jnp.einsum("mtr,mtw->mrw", grads, hid_w, preferred_element_type=jnp.float32).astype(
        jnp.bfloat16
    )
    block_range = jnp.arange(blocks, dtype=jnp.int32)[None, :]
    selector = jnp.where(
        (live_flags[:, None] > 0) & (block_ids[:, None] == block_range), 1.0, 0.0
    ).astype(jnp.bfloat16)
    grad_head = jnp.einsum("mb,mrw->brw", selector, contrib, preferred_element_type=jnp.float32)
    grad_head = grad_head.astype(jnp.bfloat16).reshape(blocks * block_rows, col_width)
    ghid = jnp.einsum("mtr,mrw->mtw", grads, picked, preferred_element_type=jnp.float32)
    ghid = lax.psum_scatter(ghid, "section", scatter_dimension=1, tiled=True).astype(jnp.bfloat16)
    ghid = lax.all_to_all(ghid, "dp", split_axis=0, concat_axis=2, tiled=True)
    grad_hidden = ghid.reshape(1, tok_local, model_width)
    return (grad_hidden, grad_head)


def solution(mesh):
    placed = (
        P("dp", "section", None),
        P("section", "dp"),
        P(None, "section"),
        P(None, "section"),
        P("dp", None, "section"),
    )
    return jax.shard_map(
        local,
        mesh=mesh,
        in_specs=placed,
        out_specs=(P("dp", "section", None), P("section", "dp")),
        check_vma=False,
    )
```

profile of v0, /device:TPU:1, one launch (start us, length us, event | category | flops | bytes accessed | tf_op | source)
XLA Modules:
  0.0 412.9 jit_solution(15351352990721341709)
XLA Ops:
  7.2 1.0 copy.29
  8.2 21.6 %all_to_all.36 = bf16[1,16,16,512]{3,1,0,2:T(8,128)(2,1)} all-to-all(bf16[1,16,16,512]{3,1,0,2:T(8,128)(2,1)S(1)} %bitcast.54), channel_id=1, replica_groups=mesh['section'=16,'dp'=16] {'dp'}, dimensions={2} | all-to-all | bytes 524288 | tf_op jit(solution)/shard_map/all_to_all | solution.py:22
  29.8 0.7 fusion.34
  30.5 7.0 %gather_fusion = bf16[16,512,512]{2,1,0:T(8,128)(2,1)} fusion(bf16[8,512,512]{2,1,0:T(8,128)(2,1)} %bitcast.50, s32[1024]{0:T(1024)S(1)} %pad_clamp_fusion), kind=kCustom, calls=%fused_computation | custom fusion | bytes 16777280 | tf_op jit(solution)/shard_map/jit(_take)/gather | solution.py:24
  37.5 45.8 %all-gather.6.cloned.1.call-done = bf16[16,1,256,1,512]{4,2,0,3,1:T(8,128)(2,1)} async-done(((bf16[16,1,16,1,512]{4,2,0,3,1:T(8,128)(2,1)}), bf16[16,1,256,1,512]{4,2,0,3,1:T(8,128)(2,1)}) %all-gather.6.cloned.1.call-update) | async-done | bytes 4194320 | tf_op jit(solution)/shard_map/all_gather | solution.py:23
  83.3 10.2 %fusion.6 = f32[16,256,512]{1,2,0:T(8,128)} fusion(bf16[16,1,256,1,512]{4,2,0,3,1:T(8,128)(2,1)} %all-gather.6.cloned.1.call-done, bf16[16,512,512]{2,1,0:T(8,128)(2,1)} %gather_fusion, pred[16]{0:T(512)(128)(4,1)S(1)} %and_bitcast_fusion), kind=kOutput, calls=%fused_computation.9 | convolution fusion | flops 2151677952 | bytes 20971536 | tf_op jit(solution)/shard_map/mtw,mrw->mtr/dot_general | solution.py:25
  93.5 0.9 copy-done
  95.9 0.6 convert_select_fusion
  96.6 64.4 %reduce-scatter.3.cloned.1.call-done = f32[1,256,512]{1,2,0:T(8,128)} async-done(((f32[16,256,512]{1,2,0:T(8,128)}), f32[1,256,512]{1,2,0:T(8,128)}) %reduce-scatter.3.cloned.1.call-update) | async-done | bytes 524304 | tf_op jit(solution)/shard_map/reduce_scatter | solution.py:26
  161.0 1.1 reduce_max.23
  162.8 33.3 %all-reduce.1 = (f32[256]{0:T(256)S(1)}, f32[256]{0:T(256)S(1)}) all-reduce(f32[256]{0:T(256)S(1)} %convert_select_fusion, f32[256]{0:T(256)S(1)} %broadcast_select_fusion.7), channel_id=1, replica_groups=mesh['section'=16,'dp'=16] {'section'}, use_global_device_ids=true, to_apply=%region_7.8 | all-reduce | flops 512 | bytes 4096 | tf_op jit(solution)/shard_map/pmax | solution.py:32
  196.2 1.2 fusion.21
  198.0 29.2 %all-reduce = (f32[256]{0:T(256)S(1)}, f32[256]{0:T(256)S(1)}, f32[]{:T(128)}) all-reduce(f32[256]{0:T(256)S(1)} %get-tuple-element.7, f32[256]{0:T(256)S(1)} %get-tuple-element.8, f32[]{:T(128)S(6)} %select_n.58), channel_id=1, replica_groups=mesh['section'=16,'dp'=16] {'section'}, use_global_device_ids=true, to_apply=%region_9.10 | all-reduce | flops 513 | bytes 4104 | tf_op jit(solution)/shard_map/psum | solution.py:35
  227.9 1.9 fusion.22
  229.8 0.8 copy.16
  230.7 54.8 %all-gather.4.cloned.1.call-done = bf16[16,256,512]{2,1,0:T(8,128)(2,1)} async-done(((bf16[1,256,512]{2,1,0:T(8,128)(2,1)}), bf16[16,256,512]{2,1,0:T(8,128)(2,1)}) %all-gather.4.cloned.1.call-update) | async-done | bytes 4194320 | tf_op jit(solution)/shard_map/all_gather | solution.py:41
  285.5 10.3 %fusion.5 = f32[16,256,512]{2,1,0:T(8,128)} fusion(bf16[16,256,512]{2,1,0:T(8,128)(2,1)} %all-gather.4.cloned.1.call-done, bf16[16,512,512]{2,1,0:T(8,128)(2,1)} %gather_fusion, pred[16]{0:T(512)(128)(4,1)S(1)} %and_bitcast_fusion), kind=kOutput, calls=%fused_computation.8 | convolution fusion | flops 2151677952 | bytes 20971536 | tf_op jit(solution)/shard_map/mtr,mrw->mtw/dot_general | solution.py:51
  295.8 9.1 %convolution_convert_fusion = bf16[16,512,512]{2,1,0:T(8,128)(2,1)} fusion(bf16[16,256,512]{2,1,0:T(8,128)(2,1)} %all-gather.4.cloned.1.call-done, bf16[16,1,256,1,512]{4,2,0,3,1:T(8,128)(2,1)} %all-gather.6.cloned.1.call-done), kind=kOutput, calls=%fused_computation.4 | convolution fusion | flops 2151677952 | bytes 16777216 | tf_op jit(solution)/shard_map/mtr,mtw->mrw/dot_general | solution.py:42
  304.9 78.3 %reduce-scatter.5.cloned.1.call-done = f32[16,16,512]{2,1,0:T(8,128)} async-done(((f32[16,256,512]{2,1,0:T(8,128)}), f32[16,16,512]{2,1,0:T(8,128)}) %reduce-scatter.5.cloned.1.call-update) | async-done | bytes 524304 | tf_op jit(solution)/shard_map/reduce_scatter | solution.py:52
  383.2 1.8 convert_element_type.29
  385.0 9.0 %all-to-all-start.1 = ((bf16[16,16,512]{2,1,0:T(8,128)(2,1)}), bf16[16,16,512]{2,1,0:T(8,128)(2,1)S(1)}, u32[]{:S(2)}, u32[]{:S(2)}) async-start(bf16[16,16,512]{2,1,0:T(8,128)(2,1)} %convert_element_type.29), calls=%async_computation.3 | async-start | bytes 524288 | tf_op jit(solution)/shard_map/all_to_all | solution.py:53
  393.9 8.1 %fusion.9 = bf16[8,512,512]{2,0,1:T(8,128)(2,1)S(1)} fusion(bf16[16,512,512]{2,1,0:T(8,128)(2,1)} %convolution_convert_fusion, s32[16]{0:T(128)S(1)} %bitcast.57, pred[16]{0:T(512)(128)(4,1)S(1)} %compare_bitcast_fusion), kind=kOutput, calls=%fused_computation.10 | convolution fusion | flops 69206528 | bytes 12582992 | tf_op jit(solution)/shard_map/mb,mrw->brw/dot_general | solution.py:49
  402.0 3.5 copy.20
  405.6 0.7 copy.23
  (23 shorter events, 2.7 us)
Async XLA Ops:
  7.2 76.1 %all-gather.6.cloned.1.call-start = ((), (), s32[]{:S(2)}) async-start(), calls=%async_computation.7 | async-start | bytes 4456448 | tf_op jit(solution)/shard_map/all_gather | solution.py:23
  29.8 131.2 %reduce-scatter.3.cloned.1.call-start = ((), (), s32[]{:S(2)}) async-start(), calls=%async_computation.4 | async-start | bytes 8912896 | tf_op jit(solution)/shard_map/reduce_scatter | solution.py:26
  30.5 7.0 %copy-start.1 = (s32[16,1]{0,1:T(1,128)S(1)}, s32[16,1]{0,1:T(1,128)}, u32[]{:S(2)}) copy-start(s32[16,1]{0,1:T(1,128)} %param.7) | copy-start | bytes 196
  93.5 0.9 copy-start
  93.5 1.2 copy-start.2
  93.5 192.0 %all-gather.4.cloned.1.call-start = ((), (), s32[]{:S(2)}) async-start(), calls=%async_computation.5 | async-start | bytes 4456448 | tf_op jit(solution)/shard_map/all_gather | solution.py:41
  230.7 152.5 %reduce-scatter.5.cloned.1.call-start = ((), (), s32[]{:S(2)}) async-start(), calls=%async_computation.6 | async-start | bytes 8912896 | tf_op jit(solution)/shard_map/reduce_scatter | solution.py:52
  385.0 20.7 %all-to-all-start.1 = ((bf16[16,16,512]{2,1,0:T(8,128)(2,1)}), bf16[16,16,512]{2,1,0:T(8,128)(2,1)S(1)}, u32[]{:S(2)}, u32[]{:S(2)}) async-start(bf16[16,16,512]{2,1,0:T(8,128)(2,1)} %convert_element_type.29), calls=%async_computation.3 | async-start | bytes 524288 | tf_op jit(solution)/shard_map/all_to_all | solution.py:53
Sparse Core Ops, SparseCore 0:
  29.9 53.3 all-gather.5
  93.6 67.3 reduce-scatter.2
  230.8 54.6 all-gather.3
  295.9 87.1 reduce-scatter.4
where the time goes:
time: 413 us
  waiting for transfers between devices  243 us (59%)
  blocking collectives  84.1 us (20%)
  matrix products  37.7 us (9%)
  between operations  15.1 us (4%)
  local copies, waits for them, and re-layouts  14 us (3%)
  other arithmetic  9.45 us (2%)
  starting transfers between devices  9.12 us (2%)
    reduce_scatter x1, waiting for transfers between devices, local(): lax.psum_scatter(ghid, 'section', scatter_dimension=1, tiled=True)  78.3 us
    reduce_scatter x1, waiting for transfers between devices, local(): logits = lax.psum_scatter(part, 'dp', scatter_dimension=0, tiled=True)[0]  64.4 us
    all_gather x1, waiting for transfers between devices, local(): grads = lax.all_gather(logit_grad[None], 'dp', axis=0, tiled=True)  54.8 us
    all_gather x1, waiting for transfers between devices, local(): lax.all_gather(pieces, 'section', axis=1, tiled=True)  45.8 us
    pmax x1, blocking collectives, local(): stud_top, teach_top = lax.pmax((stud_local, teach_local), 'section')  33.3 us
    psum x1, blocking collectives, local(): lax.psum((stud_part, teach_part, live_value), 'section')  29.2 us
    all_to_all x1, blocking collectives, local(): lax.all_to_all(pieces, 'dp', split_axis=2, concat_axis=0, tiled=True)  21.6 us
    dot_general x1, matrix products, local(): jnp.einsum('mtr,mrw->mtw', grads, picked, preferred_element_type=jnp.floa...  10.3 us
  transfers between devices with their start and end apart: 5, of which 5 were waited for; matrix products, arithmetic and copies ran while one was open for 7% of the time, Pallas kernels for 0%

commit v1 on v0

--- a/solution.py
+++ b/solution.py
@@ -4,6 +4,12 @@
 from jax.sharding import PartitionSpec as P
 
 neg_fill = -1e30
+
+
+def gather_by_exchange(x, axis, dim):
+    size = lax.axis_size(axis)
+    repeats = [size if d == dim else 1 for d in range(x.ndim)]
+    return lax.all_to_all(jnp.tile(x, repeats), axis, split_axis=dim, concat_axis=dim, tiled=True)
 
 
 def local(hidden, head, block_id, block_live, teacher):
@@ -20,7 +26,7 @@
     n_mb = block_ids.shape[0]
     pieces = hidden.reshape(1, tok_local, n_dp, col_width)
     pieces = lax.all_to_all(pieces, "dp", split_axis=2, concat_axis=0, tiled=True)
-    hid_w = lax.all_gather(pieces, "section", axis=1, tiled=True).reshape(n_mb, -1, col_width)
+    hid_w = gather_by_exchange(pieces, "section", 1).reshape(n_mb, -1, col_width)
     picked = jnp.take(table, block_ids, axis=0)
     part = jnp.einsum("mtw,mrw->mtr", hid_w, picked, preferred_element_type=jnp.float32)
     logits = lax.psum_scatter(part, "dp", scatter_dimension=0, tiled=True)[0]

time: 413 us -> 429 us (1.039)
  starting transfers between devices: 9.12 us -> 16 us
    all_to_all x0 -> x1, waiting for transfers between devices: none -> 58.4 us  [gather_by_exchange(): lax.all_to_all(jnp.tile(x, repeats), axis, split_axis=dim, concat_axis=di...]
    all_gather x1 -> x0, waiting for transfers between devices: 45.8 us -> none  [local(): lax.all_gather(pieces, 'section', axis=1, tiled=True)]
    all_to_all x0 -> x1, starting transfers between devices: none -> 6.81 us  [gather_by_exchange(): lax.all_to_all(jnp.tile(x, repeats), axis, split_axis=dim, concat_axis=di...]
    reduce_scatter x1, waiting for transfers between devices: 64.4 us -> 57.8 us  [local(): logits = lax.psum_scatter(part, 'dp', scatter_dimension=0, tiled=True)[0]]
  transfers between devices with their start and end apart: 5 -> 5, of which waited for: 5 -> 5; matrix products, arithmetic and copies ran while one was open for 7% -> 8% of each run, Pallas kernels for 0% -> 0%
where the time goes in v1:
time: 429 us; the launch traced here: 428 us
  waiting for transfers between devices  246 us (57%)
  blocking collectives  84 us (20%)
  matrix products  41.8 us (10%)
  local copies, waits for them, and re-layouts  16.7 us (4%)
  starting transfers between devices  16 us (4%)
  between operations  15.2 us (4%)
  other arithmetic  8.79 us (2%)
    reduce_scatter x1, waiting for transfers between devices, local(): lax.psum_scatter(ghid, 'section', scatter_dimension=1, tiled=True)  74.9 us
    all_to_all x1, waiting for transfers between devices, gather_by_exchange(): lax.all_to_all(jnp.tile(x, repeats), axis, split_axis=dim, concat_axis=di...  58.4 us
    reduce_scatter x1, waiting for transfers between devices, local(): logits = lax.psum_scatter(part, 'dp', scatter_dimension=0, tiled=True)[0]  57.8 us
    all_gather x1, waiting for transfers between devices, local(): grads = lax.all_gather(logit_grad[None], 'dp', axis=0, tiled=True)  54.7 us
    pmax x1, blocking collectives, local(): stud_top, teach_top = lax.pmax((stud_local, teach_local), 'section')  33.3 us
    psum x1, blocking collectives, local(): lax.psum((stud_part, teach_part, live_value), 'section')  29.2 us
    all_to_all x1, blocking collectives, local(): lax.all_to_all(pieces, 'dp', split_axis=2, concat_axis=0, tiled=True)  21.5 us
    dot_general x1, matrix products, local(): jnp.einsum('mtr,mtw->mrw', grads, hid_w, preferred_element_type=jnp.float32)  12.2 us
  transfers between devices with their start and end apart: 5, of which 5 were waited for; matrix products, arithmetic and copies ran while one was open for 8% of the time, Pallas kernels for 0%

profile of v1, /device:TPU:1, one launch (start us, length us, event | category | flops | bytes accessed | tf_op | source)
XLA Modules:
  0.0 428.3 jit_solution(14484752332999200372)
XLA Ops:
  7.2 1.0 copy.50
  8.2 21.5 %all_to_all.38 = bf16[1,16,16,512]{3,1,0,2:T(8,128)(2,1)S(1)} all-to-all(bf16[1,16,16,512]{3,1,0,2:T(8,128)(2,1)S(1)} %bitcast.58), channel_id=1, replica_groups=mesh['section'=16,'dp'=16] {'dp'}, dimensions={2} | all-to-all | bytes 524288 | tf_op jit(solution)/shard_map/all_to_all | solution.py:28
  29.8 2.5 tile.12
  32.3 6.8 %all-to-all-start.1 = ((bf16[16,256,1,512]{3,0,2,1:T(8,128)(2,1)}), bf16[16,256,1,512]{3,0,2,1:T(8,128)(2,1)}, u32[]{:S(2)}, u32[]{:S(2)}) async-start(bf16[16,256,1,512]{3,0,2,1:T(8,128)(2,1)} %bitcast.54), calls=%async_computation.1 | async-start | bytes 8388608 | tf_op jit(solution)/shard_map/all_to_all | solution.py:12
  39.2 7.0 %gather_fusion = bf16[16,512,512]{2,1,0:T(8,128)(2,1)} fusion(bf16[8,512,512]{2,1,0:T(8,128)(2,1)} %bitcast.53, s32[1024]{0:T(1024)S(1)} %pad_clamp_fusion), kind=kCustom, calls=%fused_computation | custom fusion | bytes 16777280 | tf_op jit(solution)/shard_map/jit(_take)/gather | solution.py:30
  46.2 58.4 %all-to-all-done.1 = bf16[16,256,1,512]{3,0,2,1:T(8,128)(2,1)} async-done(((bf16[16,256,1,512]{3,0,2,1:T(8,128)(2,1)}), bf16[16,256,1,512]{3,0,2,1:T(8,128)(2,1)}, u32[]{:S(2)}, u32[]{:S(2)}) %all-to-all-start.1) | async-done | bytes 4194336 | tf_op jit(solution)/shard_map/all_to_all | solution.py:12
  104.6 11.1 %fusion.8 = f32[16,256,512]{1,2,0:T(8,128)} fusion(bf16[16,256,1,512]{3,0,2,1:T(8,128)(2,1)} %all-to-all-done.1, bf16[16,512,512]{2,1,0:T(8,128)(2,1)} %gather_fusion, pred[16]{0:T(512)(128)(4,1)S(1)} %and_bitcast_fusion), kind=kOutput, calls=%fused_computation.11 | convolution fusion | flops 2151677952 | bytes 20971536 | tf_op jit(solution)/shard_map/mtw,mrw->mtr/dot_general | solution.py:31
  115.8 0.9 copy-done
  118.8 57.8 %reduce-scatter.3.cloned.1.call-done = f32[1,256,512]{1,2,0:T(8,128)} async-done(((f32[16,256,512]{1,2,0:T(8,128)}), f32[1,256,512]{1,2,0:T(8,128)}) %reduce-scatter.3.cloned.1.call-update) | async-done | bytes 524304 | tf_op jit(solution)/shard_map/reduce_scatter | solution.py:32
  176.6 1.1 reduce_max.23
  178.4 33.3 %all-reduce.1 = (f32[256]{0:T(256)S(1)}, f32[256]{0:T(256)S(1)}) all-reduce(f32[256]{0:T(256)S(1)} %convert_select_fusion, f32[256]{0:T(256)S(1)} %broadcast_select_fusion.7), channel_id=1, replica_groups=mesh['section'=16,'dp'=16] {'section'}, use_global_device_ids=true, to_apply=%region_7.8 | all-reduce | flops 512 | bytes 4096 | tf_op jit(solution)/shard_map/pmax | solution.py:38
  211.8 1.2 fusion.23
  213.6 29.2 %all-reduce = (f32[256]{0:T(256)S(1)}, f32[256]{0:T(256)S(1)}, f32[]{:T(128)}) all-reduce(f32[256]{0:T(256)S(1)} %get-tuple-element.7, f32[256]{0:T(256)S(1)} %get-tuple-element.8, f32[]{:T(128)S(6)} %select_n.58), channel_id=1, replica_groups=mesh['section'=16,'dp'=16] {'section'}, use_global_device_ids=true, to_apply=%region_9.10 | all-reduce | flops 513 | bytes 4104 | tf_op jit(solution)/shard_map/psum | solution.py:41
  243.5 1.9 fusion.24
  245.4 0.8 copy.27
  246.5 54.7 %all-gather.2.cloned.1.call-done = bf16[16,256,512]{2,1,0:T(8,128)(2,1)} async-done(((bf16[1,256,512]{2,1,0:T(8,128)(2,1)}), bf16[16,256,512]{2,1,0:T(8,128)(2,1)}) %all-gather.2.cloned.1.call-update) | async-done | bytes 4194320 | tf_op jit(solution)/shard_map/all_gather | solution.py:47
  301.2 10.3 %fusion.7 = f32[16,256,512]{2,1,0:T(8,128)} fusion(bf16[16,256,512]{2,1,0:T(8,128)(2,1)} %all-gather.2.cloned.1.call-done, bf16[16,512,512]{2,1,0:T(8,128)(2,1)} %gather_fusion, pred[16]{0:T(512)(128)(4,1)S(1)} %and_bitcast_fusion), kind=kOutput, calls=%fused_computation.10 | convolution fusion | flops 2151677952 | bytes 20971536 | tf_op jit(solution)/shard_map/mtr,mrw->mtw/dot_general | solution.py:57
  311.5 12.2 %convolution_convert_fusion = bf16[16,512,512]{2,1,0:T(8,128)(2,1)} fusion(bf16[16,256,512]{2,1,0:T(8,128)(2,1)} %all-gather.2.cloned.1.call-done, bf16[16,256,1,512]{3,0,2,1:T(8,128)(2,1)} %all-to-all-done.1), kind=kOutput, calls=%fused_computation.4 | convolution fusion | flops 2151677952 | bytes 16777216 | tf_op jit(solution)/shard_map/mtr,mtw->mrw/dot_general | solution.py:48
  323.7 74.9 %reduce-scatter.5.cloned.1.call-done = f32[16,16,512]{2,1,0:T(8,128)} async-done(((f32[16,256,512]{2,1,0:T(8,128)}), f32[16,16,512]{2,1,0:T(8,128)}) %reduce-scatter.5.cloned.1.call-update) | async-done | bytes 524304 | tf_op jit(solution)/shard_map/reduce_scatter | solution.py:58
  398.6 1.8 convert_element_type.29
  400.4 8.9 %all-to-all-start.2 = ((bf16[16,16,512]{2,1,0:T(8,128)(2,1)}), bf16[16,16,512]{2,1,0:T(8,128)(2,1)S(1)}, u32[]{:S(2)}, u32[]{:S(2)}) async-start(bf16[16,16,512]{2,1,0:T(8,128)(2,1)} %convert_element_type.29), calls=%async_computation.4 | async-start | bytes 524288 | tf_op jit(solution)/shard_map/all_to_all | solution.py:59
  409.3 8.1 %fusion.11 = bf16[8,512,512]{2,0,1:T(8,128)(2,1)S(1)} fusion(bf16[16,512,512]{2,1,0:T(8,128)(2,1)} %convolution_convert_fusion, s32[16]{0:T(128)S(1)} %bitcast.61, pred[16]{0:T(512)(128)(4,1)S(1)} %compare_bitcast_fusion), kind=kOutput, calls=%fused_computation.12 | convolution fusion | flops 69206528 | bytes 12582992 | tf_op jit(solution)/shard_map/mb,mrw->brw/dot_general | solution.py:55
  417.4 3.5 copy.31
  421.0 0.7 copy.34
  (24 shorter events, 3.6 us)
Async XLA Ops:
  7.2 32.0 %copy-start.1 = (s32[16,1]{0,1:T(1,128)S(1)}, s32[16,1]{0,1:T(1,128)}, u32[]{:S(2)}) copy-start(s32[16,1]{0,1:T(1,128)} %param.7) | copy-start | bytes 196
  32.3 72.2 %all-to-all-start.1 = ((bf16[16,256,1,512]{3,0,2,1:T(8,128)(2,1)}), bf16[16,256,1,512]{3,0,2,1:T(8,128)(2,1)}, u32[]{:S(2)}, u32[]{:S(2)}) async-start(bf16[16,256,1,512]{3,0,2,1:T(8,128)(2,1)} %bitcast.54), calls=%async_computation.1 | async-start | bytes 8388608 | tf_op jit(solution)/shard_map/all_to_all | solution.py:12
  39.2 137.5 %reduce-scatter.3.cloned.1.call-start = ((), (), s32[]{:S(2)}) async-start(), calls=%async_computation.5 | async-start | bytes 8912896 | tf_op jit(solution)/shard_map/reduce_scatter | solution.py:32
  115.7 0.9 copy-start
  115.7 1.2 copy-start.2
  115.7 185.4 %all-gather.2.cloned.1.call-start = ((), (), s32[]{:S(2)}) async-start(), calls=%async_computation.6 | async-start | bytes 4456448 | tf_op jit(solution)/shard_map/all_gather | solution.py:47
  246.3 152.4 %reduce-scatter.5.cloned.1.call-start = ((), (), s32[]{:S(2)}) async-start(), calls=%async_computation.7 | async-start | bytes 8912896 | tf_op jit(solution)/shard_map/reduce_scatter | solution.py:58
  400.4 20.6 %all-to-all-start.2 = ((bf16[16,16,512]{2,1,0:T(8,128)(2,1)}), bf16[16,16,512]{2,1,0:T(8,128)(2,1)S(1)}, u32[]{:S(2)}, u32[]{:S(2)}) async-start(bf16[16,16,512]{2,1,0:T(8,128)(2,1)} %convert_element_type.29), calls=%async_computation.4 | async-start | bytes 524288 | tf_op jit(solution)/shard_map/all_to_all | solution.py:59
Sparse Core Ops, SparseCore 0:
  115.9 60.6 reduce-scatter.2
  246.4 54.7 all-gather.1
  311.6 86.9 reduce-scatter.4
